TPU v7x, 128 devices: a whole 4x4x4 slice. The times are simulated.
128 devices in a mesh: date: 16 (over z, x), space: 8 (over y, core).
Axes of the slice: x: 4, y: 4, z: 4, core: 2. Of those that a mesh axis runs over, the one named last changes fastest.
Arguments:
- frames: bfloat16 [64, 2048, 1024], P('date', 'space'), may hold values from -6 to 6
- cloud_mask: int32 [64, 2048], P('date', 'space'), may hold values from 0 to 1
- qkv_weight: bfloat16 [2, 1024, 3072], replicated, may hold values from -0.1875 to 0.1875
- out_weight: bfloat16 [2, 1024, 1024], replicated, may hold values from -0.1875 to 0.1875
- norm_gain: float32 [2, 1024], replicated, may hold values from 0.1 to 1.9
- head_norm_scale: float32 [2, 1024], replicated, may hold values from 0.1 to 1.9
- decay: float32 [2, 64, 16], P(None, 'date'), as said below
Outputs:
- forecast: bfloat16 [64, 2048, 1024], P('date', 'space')
Inputs may be any that keep to these rules, and one draw needn't show every extreme that they name: `decay`: every entry lies strictly between 0 and 1.
All inputs are finite; a program needn't handle non-finite values.
Results may differ from a plain program's by a relative error of at most 0.0065.
Values may be sent and summed in bfloat16 or wider, within the bound.
No kernel may reach another device: no remote copies, remote signals or barrier semaphores. Data moves between devices by JAX's collectives and lax.ppermute only.
A program may use at most 128 MiB of HBM per device.

v0:
```python
import jax
import jax.numpy as jnp
from jax import lax
from jax.experimental import pallas as pl
from jax.experimental.pallas import tpu as pltpu
from jax.sharding import PartitionSpec as P

HEADS = 16
HEAD = 64
STACK_LEVELS = 2


def feature(u):
    return jax.nn.elu(u) + 1.0


def kv_chunks(key, value, n_dev):
    dates, tokens, width = key.shape
    per_head = n_dev // HEADS
    rows = HEAD // per_head

    block = 4 * HEAD

    def body(k_ref, v_ref, o_ref):
        for t in range(dates):
            for b in range(width // block):
                k = k_ref[t, :, b * block : (b + 1) * block]
                v = v_ref[t, :, b * block : (b + 1) * block]
                kv = lax.dot_general(
                    k, v, (((0,), (0,)), ((), ())), preferred_element_type=jnp.float32
                )
                for i in range(block // HEAD):
                    h = b * (block // HEAD) + i
                    for rb in range(per_head):
                        o_ref[h * per_head + rb, :, t * HEAD : (t + 1) * HEAD] = kv[
                            i * HEAD + rb * rows : i * HEAD + (rb + 1) * rows,
                            i * HEAD : (i + 1) * HEAD,
                        ]

    return pl.pallas_call(
        body,
        out_shape=jax.ShapeDtypeStruct((n_dev, rows, dates * HEAD), jnp.float32),
        in_specs=[pl.BlockSpec(memory_space=pltpu.VMEM), pl.BlockSpec(memory_space=pltpu.VMEM)],
        out_specs=pl.BlockSpec(memory_space=pltpu.VMEM),
    )(key, value)


def shards(frames, cloud_mask, qkv_weight, out_weight, norm_gain, head_norm_scale, decay):
    dates_here, tokens_here, width = frames.shape
    heads = HEADS
    n_space = lax.axis_size("space")
    n_date = lax.axis_size("date")
    n_dev = n_date * n_space
    everyone = ("date", "space")
    me = lax.axis_index("date") * n_space + lax.axis_index("space")
    entries = heads * HEAD * HEAD // n_dev
    per_head = n_dev // heads
    dates_all = n_date * dates_here
    to_each = jnp.repeat(jnp.transpose(decay, (2, 0, 1)), per_head, axis=0)
    from_each = lax.all_to_all(to_each, everyone, 0, 0, tiled=True)
    my_decay = from_each.reshape(n_date, n_space, STACK_LEVELS, dates_here)[:, 0]
    my_decay = jnp.transpose(my_decay, (1, 0, 2)).reshape(STACK_LEVELS, dates_all)
    pos = jnp.arange(dates_all)
    flag_f = cloud_mask.astype(jnp.float32)[:, :, None]
    def one_layer(layer, current):
        xf = current.astype(jnp.float32)
        in_msq = jnp.mean(xf * xf, -1, keepdims=True) + 1e-05
        normalized_output = (xf * lax.rsqrt(in_msq) * norm_gain[layer]).astype(jnp.bfloat16)
        flat = normalized_output.reshape(-1, width)
        proj_k = jnp.dot(flat, qkv_weight[layer, :, width : 2 * width], preferred_element_type=jnp.float32)
        key = (feature(proj_k.reshape(dates_here, tokens_here, width)) * flag_f).astype(jnp.bfloat16)
        proj_v = jnp.dot(flat, qkv_weight[layer, :, 2 * width :], preferred_element_type=jnp.float32)
        value = proj_v.reshape(dates_here, tokens_here, width).astype(jnp.bfloat16)
        pieces = lax.all_to_all(kv_chunks(key, value, n_dev), everyone, 0, 0, tiled=True)
        rows = pieces.shape[1]
        kv = pieces.reshape(n_date, n_space, rows, dates_here, HEAD).sum(1)
        kv = jnp.transpose(kv, (0, 2, 1, 3)).reshape(dates_all, entries)
        d = my_decay[layer]
        inside = (pos[None, None, :] > pos[None, :, None]) & (pos[None, None, :] <= pos[:, None, None])
        weight = jnp.prod(jnp.where(inside, d[None, None, :], 1.0), axis=2)
        weight = jnp.where(pos[None, :] <= pos[:, None], weight, 0.0)
        states = jnp.dot(weight, kv, precision=lax.Precision.HIGHEST, preferred_element_type=jnp.float32)
        proj_q = jnp.dot(flat, qkv_weight[layer, :, :width], preferred_element_type=jnp.float32)
        query = (
            feature(proj_q)
            .astype(jnp.bfloat16)
            .reshape(dates_here, tokens_here, heads, HEAD)
        )
        states, query = lax.optimization_barrier((states, query))
        state_b = states.astype(jnp.bfloat16).reshape(n_date, 1, dates_here, entries)
        outgoing = jnp.broadcast_to(state_b, (n_date, n_space, dates_here, entries)).reshape(
            n_dev, dates_here, entries
        )
        back = lax.all_to_all(outgoing, everyone, 0, 0, tiled=True)
        state_b = jnp.transpose(back, (1, 0, 2)).reshape(dates_here, heads, HEAD, HEAD)

        numer = jnp.einsum("tshe,thef->tshf", query, state_b, preferred_element_type=jnp.float32)
        head_msq = jnp.mean(numer * numer, -1, keepdims=True) + 1e-05
        numer = numer * lax.rsqrt(head_msq)
        mixed = (numer.reshape(dates_here, tokens_here, width) * head_norm_scale[layer]).astype(
            jnp.bfloat16
        )
        update = jnp.dot(
            mixed.reshape(-1, width), out_weight[layer], preferred_element_type=jnp.float32
        )
        return (xf + update.reshape(dates_here, tokens_here, width)).astype(jnp.bfloat16)

    return lax.fori_loop(0, STACK_LEVELS, one_layer, frames)


def solution(mesh):
    placed = (
        P("date", "space", None),
        P("date", "space"),
        P(),
        P(),
        P(),
        P(),
        P(None, "date", None),
    )
    return jax.shard_map(
        shards, mesh=mesh, in_specs=placed, out_specs=P("date", "space", None), check_vma=False
    )
```

profile of v0, /device:TPU:1, one launch (start us, length us, event | category | flops | bytes accessed | tf_op | source)
XLA Modules:
  0.0 179.9 jit_solution(17438012090988643129)
XLA Ops:
  1.6 11.5 %all-to-all-start.2 = ((f32[128,2,4]{2,1,0:T(2,128)}), f32[128,2,4]{2,1,0:T(2,128)S(1)}, u32[]{:S(2)}, u32[]{:S(2)}) async-start(f32[128,2,4]{2,1,0:T(2,128)} %bitcast.1), calls=%async_computation.2 | async-start | bytes 262144 | tf_op jit(solution)/shard_map/all_to_all | solution.py:60
  13.2 10.0 %all-to-all-done.2 = f32[128,2,4]{2,1,0:T(2,128)S(1)} async-done(((f32[128,2,4]{2,1,0:T(2,128)}), f32[128,2,4]{2,1,0:T(2,128)S(1)}, u32[]{:S(2)}, u32[]{:S(2)}) %all-to-all-start.2) | async-done | bytes 4128 | tf_op jit(solution)/shard_map/all_to_all | solution.py:60
  23.5 155.1 %while.15 = (s32[]{:T(128)}, bf16[4,256,1024]{2,1,0:T(8,128)(2,1)S(1)}, f32[2,64]{1,0:T(2,128)S(1)}, f32[2,1024]{1,0:T(2,128)S(1)}, bf16[2,1024,3072]{2,1,0:T(8,...) while((s32[]{:T(128)}, ...), condition=%wide.region_5.6_spmd.clone.clone, body=%wide.region_0.5_spmd.clone.clone.sunk | while | flops 8778675200 | bytes 92115976 | solution.py:108
  24.6 6.0 %fusion.88.v_ref = bf16[4,256,1024]{2,1,0:T(8,128)(2,1)} fusion(bf16[4,256,1024]{2,1,0:T(8,128)(2,1)S(1)} %fusion.86, bf16[2,1024,3072]{2,1,0:T(8,128)(2,1)} %get-tuple-element.314, s32[]{:T(128)S(6)} %copy.63), kind=kOutput, calls=%fused_computation.38.clone.1 | convolution fusion | flops 2148532224 | bytes 6291460 | tf_op jit(solution)/shard_map/while/body/eval_jaxpr/dot_general | solution.py:72
  30.6 6.6 %fusion.87.k_ref = bf16[4,256,1024]{2,1,0:T(8,128)(2,1)} fusion(bf16[4,256,1024]{2,1,0:T(8,128)(2,1)S(1)} %fusion.86, f32[4,256]{1,0:T(4,128)S(1)} %bitcast.105, bf16[2,1024,3072]{2,1,0:T(8,128)(2,1)} %get-tuple-element.314, s32[]{:T(128)S(6)} %copy.63), kind=kOutput, calls=%fused_computation.15.clone.1 | convolution fusion | flops 2153775104 | bytes 6295556 | tf_op jit(solution)/shard_map/while/body/eval_jaxpr/dot_general | solution.py:70
  37.1 4.1 %eval_jaxpr.5 = f32[128,8,256]{2,1,0:T(8,128)} custom-call(bf16[4,256,1024]{2,1,0:T(8,128)(2,1)} %fusion.87.k_ref, bf16[4,256,1024]{2,1,0:T(8,128)(2,1)} %fusion.88.v_ref), custom_call_target="tpu_custom_call" | custom-call | tf_op jit(solution)/shard_map/while/body/eval_jaxpr/pallas_call | solution.py:40
  41.2 4.1 %all-to-all-start = ((f32[128,8,256]{2,1,0:T(8,128)}), f32[128,8,256]{2,1,0:T(8,128)S(1)}, u32[]{:S(2)}, u32[]{:S(2)}) async-start(f32[128,8,256]{2,1,0:T(8,128)} %eval_jaxpr.5), calls=%async_computation | async-start | bytes 2097152 | tf_op jit(solution)/shard_map/while/body/eval_jaxpr/all_to_all | solution.py:74
  45.4 7.0 %fusion.91 = bf16[1024,1024]{1,0:T(8,128)(2,1)} fusion(bf16[1024,1024]{1,0:T(8,128)(2,1)} %bitcast.97, bf16[2,1024,3072]{2,1,0:T(8,128)(2,1)} %get-tuple-element.314, s32[]{:T(128)S(6)} %copy.63), kind=kOutput, calls=%fused_computation.18.clone.1 | convolution fusion | flops 2152726528 | bytes 6291460 | tf_op jit(solution)/shard_map/while/body/eval_jaxpr/dot_general | solution.py:83
  52.3 3.9 %copy.59 = bf16[1024,1024]{0,1:T(8,128)(2,1)} copy(bf16[1024,1024]{1,0:T(8,128)(2,1)} %fusion.91) | data formatting | bytes 4194304 | tf_op jit(solution)/shard_map/while/body/eval_jaxpr/convert_element_type | solution.py:86
  56.3 4.5 %reshape.210 = bf16[4,256,16,64]{1,0,3,2:T(4,128)(2,1)} reshape(bf16[1024,1024]{0,1:T(8,128)(2,1)} %copy.59) | data formatting | bytes 4194304 | tf_op jit(solution)/shard_map/while/body/eval_jaxpr/reshape | solution.py:87
  61.9 2.2 %all-to-all-done = f32[128,8,256]{2,1,0:T(8,128)S(1)} async-done(((f32[128,8,256]{2,1,0:T(8,128)}), f32[128,8,256]{2,1,0:T(8,128)S(1)}, u32[]{:S(2)}, u32[]{:S(2)}) %all-to-all-start) | async-done | bytes 1048608 | tf_op jit(solution)/shard_map/while/body/eval_jaxpr/all_to_all | solution.py:74
  64.1 2.2 %reshape.208 = f32[16,8,8,4,64]{4,3,2,1,0:T(4,128)} reshape(f32[128,8,256]{2,1,0:T(8,128)S(1)} %all-to-all-done) | data formatting | bytes 2097152 | tf_op jit(solution)/shard_map/while/body/eval_jaxpr/reshape | solution.py:76
  66.3 2.2 %reduce_sum.52 = f32[16,8,4,64]{3,2,1,0:T(4,128)S(1)} reduce(f32[16,8,8,4,64]{4,3,2,1,0:T(4,128)} %reshape.208, f32[]{:T(128)} %constant.71.clone.11..sunk), dimensions={1}, to_apply=%region_3.3 | reduce | flops 229376 | bytes 1179652 | tf_op jit(solution)/shard_map/while/body/eval_jaxpr/reduce_sum | solution.py:76
  69.9 7.6 %all-to-all-start.1 = ((bf16[128,4,512]{2,1,0:T(4,128)(2,1)}), bf16[128,4,512]{2,1,0:T(4,128)(2,1)S(1)}, u32[]{:S(2)}, u32[]{:S(2)}) async-start(bf16[128,4,512]{2,1,0:T(4,128)(2,1)} %bitcast.94), calls=%async_computation.1 | async-start | bytes 1048576 | tf_op jit(solution)/shard_map/while/body/eval_jaxpr/all_to_all | solution.py:94
  77.6 13.5 %all-to-all-done.1 = bf16[128,4,512]{2,1,0:T(4,128)(2,1)S(1)} async-done(((bf16[128,4,512]{2,1,0:T(4,128)(2,1)}), bf16[128,4,512]{2,1,0:T(4,128)(2,1)S(1)}, u32[]{:S(2)}, u32[]{:S(2)}) %all-to-all-start.1) | async-done | bytes 524320 | tf_op jit(solution)/shard_map/while/body/eval_jaxpr/all_to_all | solution.py:94
  93.6 2.5 %fusion.92 = (f32[4,256,16]{1,2,0:T(8,128)S(1)}, f32[4,16,64,256]{3,2,1,0:T(8,128)S(1)}) fusion(bf16[4,16,64,64]{3,2,1,0:T(8,128)(2,1)S(1)} %reshape.211, bf16[4,256,16,64]{1,0,3,2:T(4,128)(2,1)} %reshape.210), kind=kOutput, calls=%fused_computation.21.clone.1 | convolution fusion | flops 136298496 | bytes 6881280 | tf_op jit(solution)/shard_map/while/body/eval_jaxpr/tshe,thef->tshf/dot_general | solution.py:97
  96.7 1.7 copy-done.7
  98.3 2.5 %fusion.94 = bf16[4,256,1024]{2,1,0:T(8,128)(2,1)S(1)} fusion(bf16[4,256,1024]{2,1,0:T(8,128)(2,1)S(1)} %get-tuple-element.301, bf16[4,256,1024]{1,2,0:T(8,128)(2,1)S(1)} %bitcast.98, bf16[2,1024,1024]{2,1,0:T(8,128)(2,1)S(1)} %copy-done.7, s32[]{:T(128)S(6)} %copy.63), kind=kOutput, calls=%fused_computation.11.clone.1 | convolution fusion | flops 2150629376 | bytes 8388612 | tf_op jit(solution)/shard_map/while/body/eval_jaxpr/dot_general | solution.py:103
  101.9 6.0 %fusion.88.v_ref = bf16[4,256,1024]{2,1,0:T(8,128)(2,1)} fusion(bf16[4,256,1024]{2,1,0:T(8,128)(2,1)S(1)} %fusion.86, bf16[2,1024,3072]{2,1,0:T(8,128)(2,1)} %get-tuple-element.314, s32[]{:T(128)S(6)} %copy.63), kind=kOutput, calls=%fused_computation.38.clone.1 | convolution fusion | flops 2148532224 | bytes 6291460 | tf_op jit(solution)/shard_map/while/body/eval_jaxpr/dot_general | solution.py:72
  107.9 6.6 %fusion.87.k_ref = bf16[4,256,1024]{2,1,0:T(8,128)(2,1)} fusion(bf16[4,256,1024]{2,1,0:T(8,128)(2,1)S(1)} %fusion.86, f32[4,256]{1,0:T(4,128)S(1)} %bitcast.105, bf16[2,1024,3072]{2,1,0:T(8,128)(2,1)} %get-tuple-element.314, s32[]{:T(128)S(6)} %copy.63), kind=kOutput, calls=%fused_computation.15.clone.1 | convolution fusion | flops 2153775104 | bytes 6295556 | tf_op jit(solution)/shard_map/while/body/eval_jaxpr/dot_general | solution.py:70
  114.5 4.1 %eval_jaxpr.5 = f32[128,8,256]{2,1,0:T(8,128)} custom-call(bf16[4,256,1024]{2,1,0:T(8,128)(2,1)} %fusion.87.k_ref, bf16[4,256,1024]{2,1,0:T(8,128)(2,1)} %fusion.88.v_ref), custom_call_target="tpu_custom_call" | custom-call | tf_op jit(solution)/shard_map/while/body/eval_jaxpr/pallas_call | solution.py:40
  118.6 4.5 %all-to-all-start = ((f32[128,8,256]{2,1,0:T(8,128)}), f32[128,8,256]{2,1,0:T(8,128)S(1)}, u32[]{:S(2)}, u32[]{:S(2)}) async-start(f32[128,8,256]{2,1,0:T(8,128)} %eval_jaxpr.5), calls=%async_computation | async-start | bytes 2097152 | tf_op jit(solution)/shard_map/while/body/eval_jaxpr/all_to_all | solution.py:74
  123.1 7.0 %fusion.91 = bf16[1024,1024]{1,0:T(8,128)(2,1)} fusion(bf16[1024,1024]{1,0:T(8,128)(2,1)} %bitcast.97, bf16[2,1024,3072]{2,1,0:T(8,128)(2,1)} %get-tuple-element.314, s32[]{:T(128)S(6)} %copy.63), kind=kOutput, calls=%fused_computation.18.clone.1 | convolution fusion | flops 2152726528 | bytes 6291460 | tf_op jit(solution)/shard_map/while/body/eval_jaxpr/dot_general | solution.py:83
  130.1 3.9 %copy.59 = bf16[1024,1024]{0,1:T(8,128)(2,1)} copy(bf16[1024,1024]{1,0:T(8,128)(2,1)} %fusion.91) | data formatting | bytes 4194304 | tf_op jit(solution)/shard_map/while/body/eval_jaxpr/convert_element_type | solution.py:86
  134.0 4.5 %reshape.210 = bf16[4,256,16,64]{1,0,3,2:T(4,128)(2,1)} reshape(bf16[1024,1024]{0,1:T(8,128)(2,1)} %copy.59) | data formatting | bytes 4194304 | tf_op jit(solution)/shard_map/while/body/eval_jaxpr/reshape | solution.py:87
  139.7 2.2 %all-to-all-done = f32[128,8,256]{2,1,0:T(8,128)S(1)} async-done(((f32[128,8,256]{2,1,0:T(8,128)}), f32[128,8,256]{2,1,0:T(8,128)S(1)}, u32[]{:S(2)}, u32[]{:S(2)}) %all-to-all-start) | async-done | bytes 1048608 | tf_op jit(solution)/shard_map/while/body/eval_jaxpr/all_to_all | solution.py:74
  141.9 2.2 %reshape.208 = f32[16,8,8,4,64]{4,3,2,1,0:T(4,128)} reshape(f32[128,8,256]{2,1,0:T(8,128)S(1)} %all-to-all-done) | data formatting | bytes 2097152 | tf_op jit(solution)/shard_map/while/body/eval_jaxpr/reshape | solution.py:76
  144.1 2.2 %reduce_sum.52 = f32[16,8,4,64]{3,2,1,0:T(4,128)S(1)} reduce(f32[16,8,8,4,64]{4,3,2,1,0:T(4,128)} %reshape.208, f32[]{:T(128)} %constant.71.clone.11..sunk), dimensions={1}, to_apply=%region_3.3 | reduce | flops 229376 | bytes 1179652 | tf_op jit(solution)/shard_map/while/body/eval_jaxpr/reduce_sum | solution.py:76
  147.7 7.6 %all-to-all-start.1 = ((bf16[128,4,512]{2,1,0:T(4,128)(2,1)}), bf16[128,4,512]{2,1,0:T(4,128)(2,1)S(1)}, u32[]{:S(2)}, u32[]{:S(2)}) async-start(bf16[128,4,512]{2,1,0:T(4,128)(2,1)} %bitcast.94), calls=%async_computation.1 | async-start | bytes 1048576 | tf_op jit(solution)/shard_map/while/body/eval_jaxpr/all_to_all | solution.py:94
  155.4 13.5 %all-to-all-done.1 = bf16[128,4,512]{2,1,0:T(4,128)(2,1)S(1)} async-done(((bf16[128,4,512]{2,1,0:T(4,128)(2,1)}), bf16[128,4,512]{2,1,0:T(4,128)(2,1)S(1)}, u32[]{:S(2)}, u32[]{:S(2)}) %all-to-all-start.1) | async-done | bytes 524320 | tf_op jit(solution)/shard_map/while/body/eval_jaxpr/all_to_all | solution.py:94
  171.4 2.5 %fusion.92 = (f32[4,256,16]{1,2,0:T(8,128)S(1)}, f32[4,16,64,256]{3,2,1,0:T(8,128)S(1)}) fusion(bf16[4,16,64,64]{3,2,1,0:T(8,128)(2,1)S(1)} %reshape.211, bf16[4,256,16,64]{1,0,3,2:T(4,128)(2,1)} %reshape.210), kind=kOutput, calls=%fused_computation.21.clone.1 | convolution fusion | flops 136298496 | bytes 6881280 | tf_op jit(solution)/shard_map/while/body/eval_jaxpr/tshe,thef->tshf/dot_general | solution.py:97
  176.1 2.5 %fusion.94 = bf16[4,256,1024]{2,1,0:T(8,128)(2,1)S(1)} fusion(bf16[4,256,1024]{2,1,0:T(8,128)(2,1)S(1)} %get-tuple-element.301, bf16[4,256,1024]{1,2,0:T(8,128)(2,1)S(1)} %bitcast.98, bf16[2,1024,1024]{2,1,0:T(8,128)(2,1)S(1)} %copy-done.7, s32[]{:T(128)S(6)} %copy.63), kind=kOutput, calls=%fused_computation.11.clone.1 | convolution fusion | flops 2150629376 | bytes 8388612 | tf_op jit(solution)/shard_map/while/body/eval_jaxpr/dot_general | solution.py:103
  (62 shorter events, 18.3 us)
Async XLA Ops:
  0.0 23.4 %copy-start.1 = (bf16[4,256,1024]{2,1,0:T(8,128)(2,1)S(1)}, bf16[4,256,1024]{2,1,0:T(8,128)(2,1)}, u32[]{:S(2)}) copy-start(bf16[4,256,1024]{2,1,0:T(8,128)(2,1)} %param.9) | copy-start | bytes 6291460
  0.0 13.1 %copy-start.6 = (s32[4,256]{1,0:T(4,128)S(1)}, s32[4,256]{1,0:T(4,128)}, u32[]{:S(2)}) copy-start(s32[4,256]{1,0:T(4,128)} %param.10) | copy-start | bytes 12292
  0.0 23.4 %copy-start.3 = (f32[2,1024]{1,0:T(2,128)S(1)}, f32[2,1024]{1,0:T(2,128)}, u32[]{:S(2)}) copy-start(f32[2,1024]{1,0:T(2,128)} %param.13) | copy-start | bytes 24580
  0.0 23.4 %copy-start.4 = (f32[2,1024]{1,0:T(2,128)S(1)}, f32[2,1024]{1,0:T(2,128)}, u32[]{:S(2)}) copy-start(f32[2,1024]{1,0:T(2,128)} %param.14) | copy-start | bytes 24580
  0.0 0.8 copy-start.5
  1.6 21.5 %all-to-all-start.2 = ((f32[128,2,4]{2,1,0:T(2,128)}), f32[128,2,4]{2,1,0:T(2,128)S(1)}, u32[]{:S(2)}, u32[]{:S(2)}) async-start(f32[128,2,4]{2,1,0:T(2,128)} %bitcast.1), calls=%async_computation.2 | async-start | bytes 262144 | tf_op jit(solution)/shard_map/all_to_all | solution.py:60
  24.5 6.0 %copy-start.2 = (bf16[4,256,1024]{2,1,0:T(8,128)(2,1)}, bf16[4,256,1024]{2,1,0:T(8,128)(2,1)S(1)}, u32[]{:S(2)}) copy-start(bf16[4,256,1024]{2,1,0:T(8,128)(2,1)S(1)} %fusion.86) | copy-start | bytes 6291460 | tf_op jit(solution)/shard_map/while
  41.2 22.9 %all-to-all-start = ((f32[128,8,256]{2,1,0:T(8,128)}), f32[128,8,256]{2,1,0:T(8,128)S(1)}, u32[]{:S(2)}, u32[]{:S(2)}) async-start(f32[128,8,256]{2,1,0:T(8,128)} %eval_jaxpr.5), calls=%async_computation | async-start | bytes 2097152 | tf_op jit(solution)/shard_map/while/body/eval_jaxpr/all_to_all | solution.py:74
  69.9 21.1 %all-to-all-start.1 = ((bf16[128,4,512]{2,1,0:T(4,128)(2,1)}), bf16[128,4,512]{2,1,0:T(4,128)(2,1)S(1)}, u32[]{:S(2)}, u32[]{:S(2)}) async-start(bf16[128,4,512]{2,1,0:T(4,128)(2,1)} %bitcast.94), calls=%async_computation.1 | async-start | bytes 1048576 | tf_op jit(solution)/shard_map/while/body/eval_jaxpr/all_to_all | solution.py:94
  96.1 2.2 %copy-start.7 = (bf16[2,1024,1024]{2,1,0:T(8,128)(2,1)S(1)}, bf16[2,1024,1024]{2,1,0:T(8,128)(2,1)}, u32[]{:S(2)}) copy-start(bf16[2,1024,1024]{2,1,0:T(8,128)(2,1)} %get-tuple-element.317) | copy-start | bytes 12582916 | tf_op jit(solution)/shard_map/while
  101.9 6.0 %copy-start.2 = (bf16[4,256,1024]{2,1,0:T(8,128)(2,1)}, bf16[4,256,1024]{2,1,0:T(8,128)(2,1)S(1)}, u32[]{:S(2)}) copy-start(bf16[4,256,1024]{2,1,0:T(8,128)(2,1)S(1)} %fusion.86) | copy-start | bytes 6291460 | tf_op jit(solution)/shard_map/while
  118.6 23.4 %all-to-all-start = ((f32[128,8,256]{2,1,0:T(8,128)}), f32[128,8,256]{2,1,0:T(8,128)S(1)}, u32[]{:S(2)}, u32[]{:S(2)}) async-start(f32[128,8,256]{2,1,0:T(8,128)} %eval_jaxpr.5), calls=%async_computation | async-start | bytes 2097152 | tf_op jit(solution)/shard_map/while/body/eval_jaxpr/all_to_all | solution.py:74
  147.7 21.1 %all-to-all-start.1 = ((bf16[128,4,512]{2,1,0:T(4,128)(2,1)}), bf16[128,4,512]{2,1,0:T(4,128)(2,1)S(1)}, u32[]{:S(2)}, u32[]{:S(2)}) async-start(bf16[128,4,512]{2,1,0:T(4,128)(2,1)} %bitcast.94), calls=%async_computation.1 | async-start | bytes 1048576 | tf_op jit(solution)/shard_map/while/body/eval_jaxpr/all_to_all | solution.py:94
  173.9 2.2 %copy-start.7 = (bf16[2,1024,1024]{2,1,0:T(8,128)(2,1)S(1)}, bf16[2,1024,1024]{2,1,0:T(8,128)(2,1)}, u32[]{:S(2)}) copy-start(bf16[2,1024,1024]{2,1,0:T(8,128)(2,1)} %get-tuple-element.317) | copy-start | bytes 12582916 | tf_op jit(solution)/shard_map/while
  178.6 1.3 copy-start
where the time goes:
time: 181 us; the launch traced here: 180 us
  matrix products  49.5 us (27%)
  waiting for transfers between devices  41.3 us (23%)
  local copies, waits for them, and re-layouts  35.3 us (20%)
  starting transfers between devices  35.3 us (20%)
  other arithmetic  9.89 us (5%)
  Pallas kernels  8.23 us (5%)
    all_to_all x2, waiting for transfers between devices, one_layer(): back = lax.all_to_all(outgoing, everyone, 0, 0, tiled=True)  26.9 us
    all_to_all x2, starting transfers between devices, one_layer(): back = lax.all_to_all(outgoing, everyone, 0, 0, tiled=True)  15.2 us
    dot_general x2, matrix products, one_layer(): jnp.dot(flat, qkv_weight[layer, :, :width], preferred_element_type=jnp.fl...  13.9 us
    dot_general x2, matrix products, one_layer(): jnp.dot(flat, qkv_weight[layer, :, width:2 * width], preferred_element_ty...  13.1 us
    dot_general x2, matrix products, one_layer(): jnp.dot(flat, qkv_weight[layer, :, 2 * width:], preferred_element_type=jn...  12 us
    all_to_all x1, starting transfers between devices, shards(): from_each = lax.all_to_all(to_each, everyone, 0, 0, tiled=True)  11.5 us
    all_to_all x1, waiting for transfers between devices, shards(): from_each = lax.all_to_all(to_each, everyone, 0, 0, tiled=True)  9.99 us
    reshape x2, local copies, waits for them, and re-layouts, one_layer(): query = feature(proj_q).astype(jnp.bfloat16).reshape(dates_here, tokens_h...  8.99 us
  transfers between devices with their start and end apart: 5, of which 5 were waited for; matrix products, arithmetic and copies ran while one was open for 19% of the time, Pallas kernels for 0%

commit v1 on v0

--- a/solution.py
+++ b/solution.py
@@ -14,14 +14,15 @@
     return jax.nn.elu(u) + 1.0
 
 
-def kv_chunks(key, value, n_dev):
+def kv_chunks(key, value, extra, n_dev):
     dates, tokens, width = key.shape
     per_head = n_dev // HEADS
     rows = HEAD // per_head
 
     block = 4 * HEAD
 
-    def body(k_ref, v_ref, o_ref):
+    def body(k_ref, v_ref, e_ref, o_ref):
+        o_ref[:, :, dates * HEAD :] = e_ref[...]
         for t in range(dates):
             for b in range(width // block):
                 k = k_ref[t, :, b * block : (b + 1) * block]
@@ -39,10 +40,12 @@
 
     return pl.pallas_call(
         body,
-        out_shape=jax.ShapeDtypeStruct((n_dev, rows, dates * HEAD), jnp.float32),
-        in_specs=[pl.BlockSpec(memory_space=pltpu.VMEM), pl.BlockSpec(memory_space=pltpu.VMEM)],
+        out_shape=jax.ShapeDtypeStruct(
+            (n_dev, rows, dates * HEAD + extra.shape[2]), jnp.float32
+        ),
+        in_specs=[pl.BlockSpec(memory_space=pltpu.VMEM)] * 3,
         out_specs=pl.BlockSpec(memory_space=pltpu.VMEM),
-    )(key, value)
+    )(key, value, extra)
 
 
 def shards(frames, cloud_mask, qkv_weight, out_weight, norm_gain, head_norm_scale, decay):
@@ -56,10 +59,9 @@
     entries = heads * HEAD * HEAD // n_dev
     per_head = n_dev // heads
     dates_all = n_date * dates_here
-    to_each = jnp.repeat(jnp.transpose(decay, (2, 0, 1)), per_head, axis=0)
-    from_each = lax.all_to_all(to_each, everyone, 0, 0, tiled=True)
-    my_decay = from_each.reshape(n_date, n_space, STACK_LEVELS, dates_here)[:, 0]
-    my_decay = jnp.transpose(my_decay, (1, 0, 2)).reshape(STACK_LEVELS, dates_all)
+    lanes = 128
+    to_each = jnp.repeat(jnp.transpose(decay, (0, 2, 1)), per_head, axis=1)
+    to_each = jnp.pad(to_each[:, :, None, :], ((0, 0), (0, 0), (0, 0), (0, lanes - dates_here)))
     pos = jnp.arange(dates_all)
     flag_f = cloud_mask.astype(jnp.float32)[:, :, None]
     def one_layer(layer, current):
@@ -71,11 +73,14 @@
         key = (feature(proj_k.reshape(dates_here, tokens_here, width)) * flag_f).astype(jnp.bfloat16)
         proj_v = jnp.dot(flat, qkv_weight[layer, :, 2 * width :], preferred_element_type=jnp.float32)
         value = proj_v.reshape(dates_here, tokens_here, width).astype(jnp.bfloat16)
-        pieces = lax.all_to_all(kv_chunks(key, value, n_dev), everyone, 0, 0, tiled=True)
+        extra = jnp.broadcast_to(to_each[layer], (n_dev, HEAD // per_head, lanes))
+        pieces = lax.all_to_all(kv_chunks(key, value, extra, n_dev), everyone, 0, 0, tiled=True)
         rows = pieces.shape[1]
+        d = pieces[:, 0, dates_here * HEAD : dates_here * HEAD + dates_here]
+        d = d.reshape(n_date, n_space, dates_here)[:, 0].reshape(dates_all)
+        pieces = pieces[:, :, : dates_here * HEAD]
         kv = pieces.reshape(n_date, n_space, rows, dates_here, HEAD).sum(1)
         kv = jnp.transpose(kv, (0, 2, 1, 3)).reshape(dates_all, entries)
-        d = my_decay[layer]
         inside = (pos[None, None, :] > pos[None, :, None]) & (pos[None, None, :] <= pos[:, None, None])
         weight = jnp.prod(jnp.where(inside, d[None, None, :], 1.0), axis=2)
         weight = jnp.where(pos[None, :] <= pos[:, None], weight, 0.0)

time: 181 us -> 183 us (1.011)
  starting transfers between devices: 35.3 us -> 27 us
  local copies, waits for them, and re-layouts: 35.3 us -> 41.6 us
  waiting for transfers between devices: 41.3 us -> 44.6 us
    all_to_all x2, starting transfers between devices: 15.2 us -> 9.66 us  [one_layer(): back = lax.all_to_all(outgoing, everyone, 0, 0, tiled=True)]
    slice x1 -> x6, local copies, waits for them, and re-layouts: 0.01 us -> 4.76 us  [the longest x2 2.59 us: one_layer(): pieces = pieces[:, :, :dates_here * HEAD]]
    all_to_all x3 -> x2, waiting for transfers between devices: 14.4 us -> 17.4 us  [one_layer(): lax.all_to_all(kv_chunks(key, value, extra, n_dev), everyone, 0, 0, tiled...]
    all_to_all x3 -> x2, starting transfers between devices: 20.1 us -> 17.3 us  [one_layer(): lax.all_to_all(kv_chunks(key, value, extra, n_dev), everyone, 0, 0, tiled...]
  transfers between devices with their start and end apart: 5 -> 4, of which waited for: 5 -> 4; matrix products, arithmetic and copies ran while one was open for 19% -> 17% of each run, Pallas kernels for 0% -> 0%
where the time goes in v1:
time: 183 us; the launch traced here: 182 us
  matrix products  49.5 us (27%)
  waiting for transfers between devices  44.6 us (24%)
  local copies, waits for them, and re-layouts  41.6 us (23%)
  starting transfers between devices  27 us (15%)
  other arithmetic  9.88 us (5%)
  Pallas kernels  8.77 us (5%)
    all_to_all x2, waiting for transfers between devices, one_layer(): back = lax.all_to_all(outgoing, everyone, 0, 0, tiled=True)  27.2 us
    all_to_all x2, waiting for transfers between devices, one_layer(): lax.all_to_all(kv_chunks(key, value, extra, n_dev), everyone, 0, 0, tiled...  17.4 us
    all_to_all x2, starting transfers between devices, one_layer(): lax.all_to_all(kv_chunks(key, value, extra, n_dev), everyone, 0, 0, tiled...  17.3 us
    dot_general x2, matrix products, one_layer(): jnp.dot(flat, qkv_weight[layer, :, :width], preferred_element_type=jnp.fl...  14 us
    dot_general x2, matrix products, one_layer(): jnp.dot(flat, qkv_weight[layer, :, width:2 * width], preferred_element_ty...  13.1 us
    dot_general x2, matrix products, one_layer(): jnp.dot(flat, qkv_weight[layer, :, 2 * width:], preferred_element_type=jn...  12 us
    all_to_all x2, starting transfers between devices, one_layer(): back = lax.all_to_all(outgoing, everyone, 0, 0, tiled=True)  9.66 us
    reshape x2, local copies, waits for them, and re-layouts, one_layer(): query = feature(proj_q).astype(jnp.bfloat16).reshape(dates_here, tokens_h...  8.99 us
  transfers between devices with their start and end apart: 4, of which 4 were waited for; matrix products, arithmetic and copies ran while one was open for 17% of the time, Pallas kernels for 0%

profile of v1, /device:TPU:1, one launch (start us, length us, event | category | flops | bytes accessed | tf_op | source)
XLA Modules:
  0.0 181.7 jit_solution(3063604286029824249)
XLA Ops:
  1.6 178.8 %while.15 = (s32[]{:T(128)}, bf16[4,256,1024]{2,1,0:T(8,128)(2,1)S(1)}, f32[2,1024]{1,0:T(2,128)S(1)}, bf16[2,1024,3072]{2,1,0:T(8,128)(2,1)}, f32[4,256,1]{1,0,...) while((s32[]{:T(128)}, ...), condition=%wide.region_5.6_spmd.clone.clone, body=%wide.region_0.5_spmd.clone.clone.sunk | while | flops 8778675200 | bytes 96511496 | solution.py:113
  2.7 6.0 %fusion.86.v_ref = bf16[4,256,1024]{2,1,0:T(8,128)(2,1)} fusion(bf16[4,256,1024]{2,1,0:T(8,128)(2,1)S(1)} %fusion.84, bf16[2,1024,3072]{2,1,0:T(8,128)(2,1)} %get-tuple-element.313, s32[]{:T(128)S(6)} %copy.52), kind=kOutput, calls=%fused_computation.38.clone.1 | convolution fusion | flops 2148532224 | bytes 6291460 | tf_op jit(solution)/shard_map/while/body/eval_jaxpr/dot_general | solution.py:74
  8.7 6.6 %fusion.85.k_ref = bf16[4,256,1024]{2,1,0:T(8,128)(2,1)} fusion(bf16[4,256,1024]{2,1,0:T(8,128)(2,1)S(1)} %fusion.84, f32[4,256]{1,0:T(4,128)S(1)} %bitcast.110, bf16[2,1024,3072]{2,1,0:T(8,128)(2,1)} %get-tuple-element.313, s32[]{:T(128)S(6)} %copy.52), kind=kOutput, calls=%fused_computation.15.clone.1 | convolution fusion | flops 2153775104 | bytes 6295556 | tf_op jit(solution)/shard_map/while/body/eval_jaxpr/dot_general | solution.py:72
  16.1 4.4 %eval_jaxpr.5 = f32[128,8,384]{2,1,0:T(8,128)} custom-call(bf16[4,256,1024]{2,1,0:T(8,128)(2,1)} %fusion.85.k_ref, bf16[4,256,1024]{2,1,0:T(8,128)(2,1)} %fusion.86.v_ref, f32[128,8,128]{2,1,0:T(8,128)} %broadcast_in_dim.135.e_ref), custom_call_target="tpu_custom_call" | custom-call | tf_op jit(solution)/shard_map/while/body/eval_jaxpr/pallas_call | solution.py:41
  20.5 11.9 %all-to-all-start = ((f32[128,8,384]{2,1,0:T(8,128)}), f32[128,8,384]{2,1,0:T(8,128)}, u32[]{:S(2)}, u32[]{:S(2)}) async-start(f32[128,8,384]{2,1,0:T(8,128)} %eval_jaxpr.5), calls=%async_computation | async-start | bytes 3145728 | tf_op jit(solution)/shard_map/while/body/eval_jaxpr/all_to_all | solution.py:77
  32.4 7.0 %fusion.88 = bf16[1024,1024]{1,0:T(8,128)(2,1)} fusion(bf16[1024,1024]{1,0:T(8,128)(2,1)} %bitcast.102, bf16[2,1024,3072]{2,1,0:T(8,128)(2,1)} %get-tuple-element.313, s32[]{:T(128)S(6)} %copy.52), kind=kOutput, calls=%fused_computation.18.clone.1 | convolution fusion | flops 2152726528 | bytes 6291460 | tf_op jit(solution)/shard_map/while/body/eval_jaxpr/dot_general | solution.py:88
  39.4 3.9 %copy.48 = bf16[1024,1024]{0,1:T(8,128)(2,1)} copy(bf16[1024,1024]{1,0:T(8,128)(2,1)} %fusion.88) | data formatting | bytes 4194304 | tf_op jit(solution)/shard_map/while/body/eval_jaxpr/convert_element_type | solution.py:91
  43.3 4.5 %reshape.197 = bf16[4,256,16,64]{1,0,3,2:T(4,128)(2,1)} reshape(bf16[1024,1024]{0,1:T(8,128)(2,1)} %copy.48) | data formatting | bytes 4194304 | tf_op jit(solution)/shard_map/while/body/eval_jaxpr/reshape | solution.py:92
  47.8 8.6 %all-to-all-done = f32[128,8,384]{2,1,0:T(8,128)} async-done(((f32[128,8,384]{2,1,0:T(8,128)}), f32[128,8,384]{2,1,0:T(8,128)}, u32[]{:S(2)}, u32[]{:S(2)}) %all-to-all-start) | async-done | bytes 1572896 | tf_op jit(solution)/shard_map/while/body/eval_jaxpr/all_to_all | solution.py:77
  59.0 2.2 %reshape.195 = f32[16,8,8,4,64]{4,3,2,1,0:T(4,128)} reshape(f32[128,8,256]{2,1,0:T(8,128)S(1)} %slice.33) | data formatting | bytes 2097152 | tf_op jit(solution)/shard_map/while/body/eval_jaxpr/reshape | solution.py:82
  61.2 2.2 %reduce_sum.52 = f32[16,8,4,64]{3,2,1,0:T(4,128)S(1)} reduce(f32[16,8,8,4,64]{4,3,2,1,0:T(4,128)} %reshape.195, f32[]{:T(128)} %constant.80.clone.1..sunk), dimensions={1}, to_apply=%region_3.3 | reduce | flops 229376 | bytes 1179652 | tf_op jit(solution)/shard_map/while/body/eval_jaxpr/reduce_sum | solution.py:82
  65.9 4.8 %all-to-all-start.1 = ((bf16[128,4,512]{2,1,0:T(4,128)(2,1)}), bf16[128,4,512]{2,1,0:T(4,128)(2,1)S(1)}, u32[]{:S(2)}, u32[]{:S(2)}) async-start(bf16[128,4,512]{2,1,0:T(4,128)(2,1)} %bitcast.99), calls=%async_computation.1 | async-start | bytes 1048576 | tf_op jit(solution)/shard_map/while/body/eval_jaxpr/all_to_all | solution.py:99
  70.8 13.6 %all-to-all-done.1 = bf16[128,4,512]{2,1,0:T(4,128)(2,1)S(1)} async-done(((bf16[128,4,512]{2,1,0:T(4,128)(2,1)}), bf16[128,4,512]{2,1,0:T(4,128)(2,1)S(1)}, u32[]{:S(2)}, u32[]{:S(2)}) %all-to-all-start.1) | async-done | bytes 524320 | tf_op jit(solution)/shard_map/while/body/eval_jaxpr/all_to_all | solution.py:99
  87.0 2.5 %fusion.89 = (f32[4,256,16]{1,2,0:T(8,128)S(1)}, f32[4,16,64,256]{3,2,1,0:T(8,128)S(1)}) fusion(bf16[4,16,64,64]{3,2,1,0:T(8,128)(2,1)S(1)} %reshape.198, bf16[4,256,16,64]{1,0,3,2:T(4,128)(2,1)} %reshape.197), kind=kOutput, calls=%fused_computation.21.clone.1 | convolution fusion | flops 136298496 | bytes 6881280 | tf_op jit(solution)/shard_map/while/body/eval_jaxpr/tshe,thef->tshf/dot_general | solution.py:102
  90.0 1.7 copy-done.7
  91.7 2.5 %fusion.91 = bf16[4,256,1024]{2,1,0:T(8,128)(2,1)S(1)} fusion(bf16[4,256,1024]{2,1,0:T(8,128)(2,1)S(1)} %get-tuple-element.301, bf16[4,256,1024]{1,2,0:T(8,128)(2,1)S(1)} %bitcast.103, bf16[2,1024,1024]{2,1,0:T(8,128)(2,1)S(1)} %copy-done.7, s32[]{:T(128)S(6)} %copy.52), kind=kOutput, calls=%fused_computation.11.clone.1 | convolution fusion | flops 2150629376 | bytes 8388612 | tf_op jit(solution)/shard_map/while/body/eval_jaxpr/dot_general | solution.py:108
  95.2 6.0 %fusion.86.v_ref = bf16[4,256,1024]{2,1,0:T(8,128)(2,1)} fusion(bf16[4,256,1024]{2,1,0:T(8,128)(2,1)S(1)} %fusion.84, bf16[2,1024,3072]{2,1,0:T(8,128)(2,1)} %get-tuple-element.313, s32[]{:T(128)S(6)} %copy.52), kind=kOutput, calls=%fused_computation.38.clone.1 | convolution fusion | flops 2148532224 | bytes 6291460 | tf_op jit(solution)/shard_map/while/body/eval_jaxpr/dot_general | solution.py:74
  101.3 6.6 %fusion.85.k_ref = bf16[4,256,1024]{2,1,0:T(8,128)(2,1)} fusion(bf16[4,256,1024]{2,1,0:T(8,128)(2,1)S(1)} %fusion.84, f32[4,256]{1,0:T(4,128)S(1)} %bitcast.110, bf16[2,1024,3072]{2,1,0:T(8,128)(2,1)} %get-tuple-element.313, s32[]{:T(128)S(6)} %copy.52), kind=kOutput, calls=%fused_computation.15.clone.1 | convolution fusion | flops 2153775104 | bytes 6295556 | tf_op jit(solution)/shard_map/while/body/eval_jaxpr/dot_general | solution.py:72
  108.7 4.4 %eval_jaxpr.5 = f32[128,8,384]{2,1,0:T(8,128)} custom-call(bf16[4,256,1024]{2,1,0:T(8,128)(2,1)} %fusion.85.k_ref, bf16[4,256,1024]{2,1,0:T(8,128)(2,1)} %fusion.86.v_ref, f32[128,8,128]{2,1,0:T(8,128)} %broadcast_in_dim.135.e_ref), custom_call_target="tpu_custom_call" | custom-call | tf_op jit(solution)/shard_map/while/body/eval_jaxpr/pallas_call | solution.py:41
  113.0 5.4 %all-to-all-start = ((f32[128,8,384]{2,1,0:T(8,128)}), f32[128,8,384]{2,1,0:T(8,128)}, u32[]{:S(2)}, u32[]{:S(2)}) async-start(f32[128,8,384]{2,1,0:T(8,128)} %eval_jaxpr.5), calls=%async_computation | async-start | bytes 3145728 | tf_op jit(solution)/shard_map/while/body/eval_jaxpr/all_to_all | solution.py:77
  118.5 7.0 %fusion.88 = bf16[1024,1024]{1,0:T(8,128)(2,1)} fusion(bf16[1024,1024]{1,0:T(8,128)(2,1)} %bitcast.102, bf16[2,1024,3072]{2,1,0:T(8,128)(2,1)} %get-tuple-element.313, s32[]{:T(128)S(6)} %copy.52), kind=kOutput, calls=%fused_computation.18.clone.1 | convolution fusion | flops 2152726528 | bytes 6291460 | tf_op jit(solution)/shard_map/while/body/eval_jaxpr/dot_general | solution.py:88
  125.5 3.9 %copy.48 = bf16[1024,1024]{0,1:T(8,128)(2,1)} copy(bf16[1024,1024]{1,0:T(8,128)(2,1)} %fusion.88) | data formatting | bytes 4194304 | tf_op jit(solution)/shard_map/while/body/eval_jaxpr/convert_element_type | solution.py:91
  129.4 4.5 %reshape.197 = bf16[4,256,16,64]{1,0,3,2:T(4,128)(2,1)} reshape(bf16[1024,1024]{0,1:T(8,128)(2,1)} %copy.48) | data formatting | bytes 4194304 | tf_op jit(solution)/shard_map/while/body/eval_jaxpr/reshape | solution.py:92
  133.9 8.8 %all-to-all-done = f32[128,8,384]{2,1,0:T(8,128)} async-done(((f32[128,8,384]{2,1,0:T(8,128)}), f32[128,8,384]{2,1,0:T(8,128)}, u32[]{:S(2)}, u32[]{:S(2)}) %all-to-all-start) | async-done | bytes 1572896 | tf_op jit(solution)/shard_map/while/body/eval_jaxpr/all_to_all | solution.py:77
  145.2 2.2 %reshape.195 = f32[16,8,8,4,64]{4,3,2,1,0:T(4,128)} reshape(f32[128,8,256]{2,1,0:T(8,128)S(1)} %slice.33) | data formatting | bytes 2097152 | tf_op jit(solution)/shard_map/while/body/eval_jaxpr/reshape | solution.py:82
  147.4 2.2 %reduce_sum.52 = f32[16,8,4,64]{3,2,1,0:T(4,128)S(1)} reduce(f32[16,8,8,4,64]{4,3,2,1,0:T(4,128)} %reshape.195, f32[]{:T(128)} %constant.80.clone.1..sunk), dimensions={1}, to_apply=%region_3.3 | reduce | flops 229376 | bytes 1179652 | tf_op jit(solution)/shard_map/while/body/eval_jaxpr/reduce_sum | solution.py:82
  152.1 4.8 %all-to-all-start.1 = ((bf16[128,4,512]{2,1,0:T(4,128)(2,1)}), bf16[128,4,512]{2,1,0:T(4,128)(2,1)S(1)}, u32[]{:S(2)}, u32[]{:S(2)}) async-start(bf16[128,4,512]{2,1,0:T(4,128)(2,1)} %bitcast.99), calls=%async_computation.1 | async-start | bytes 1048576 | tf_op jit(solution)/shard_map/while/body/eval_jaxpr/all_to_all | solution.py:99
  157.1 13.6 %all-to-all-done.1 = bf16[128,4,512]{2,1,0:T(4,128)(2,1)S(1)} async-done(((bf16[128,4,512]{2,1,0:T(4,128)(2,1)}), bf16[128,4,512]{2,1,0:T(4,128)(2,1)S(1)}, u32[]{:S(2)}, u32[]{:S(2)}) %all-to-all-start.1) | async-done | bytes 524320 | tf_op jit(solution)/shard_map/while/body/eval_jaxpr/all_to_all | solution.py:99
  171.5 1.6 reshape.198
  173.2 2.5 %fusion.89 = (f32[4,256,16]{1,2,0:T(8,128)S(1)}, f32[4,16,64,256]{3,2,1,0:T(8,128)S(1)}) fusion(bf16[4,16,64,64]{3,2,1,0:T(8,128)(2,1)S(1)} %reshape.198, bf16[4,256,16,64]{1,0,3,2:T(4,128)(2,1)} %reshape.197), kind=kOutput, calls=%fused_computation.21.clone.1 | convolution fusion | flops 136298496 | bytes 6881280 | tf_op jit(solution)/shard_map/while/body/eval_jaxpr/tshe,thef->tshf/dot_general | solution.py:102
  176.3 1.7 copy-done.7
  177.9 2.5 %fusion.91 = bf16[4,256,1024]{2,1,0:T(8,128)(2,1)S(1)} fusion(bf16[4,256,1024]{2,1,0:T(8,128)(2,1)S(1)} %get-tuple-element.301, bf16[4,256,1024]{1,2,0:T(8,128)(2,1)S(1)} %bitcast.103, bf16[2,1024,1024]{2,1,0:T(8,128)(2,1)S(1)} %copy-done.7, s32[]{:T(128)S(6)} %copy.52), kind=kOutput, calls=%fused_computation.11.clone.1 | convolution fusion | flops 2150629376 | bytes 8388612 | tf_op jit(solution)/shard_map/while/body/eval_jaxpr/dot_general | solution.py:108
  (67 shorter events, 21.3 us)
Async XLA Ops:
  0.0 1.6 copy-start.1
  0.0 1.0 copy-start.6
  0.0 1.6 copy-start.3
  0.0 1.6 copy-start.4
  0.0 0.8 copy-start.5
  2.7 6.0 %copy-start.2 = (bf16[4,256,1024]{2,1,0:T(8,128)(2,1)}, bf16[4,256,1024]{2,1,0:T(8,128)(2,1)S(1)}, u32[]{:S(2)}) copy-start(bf16[4,256,1024]{2,1,0:T(8,128)(2,1)S(1)} %fusion.84) | copy-start | bytes 6291460 | tf_op jit(solution)/shard_map/while
  20.5 36.0 %all-to-all-start = ((f32[128,8,384]{2,1,0:T(8,128)}), f32[128,8,384]{2,1,0:T(8,128)}, u32[]{:S(2)}, u32[]{:S(2)}) async-start(f32[128,8,384]{2,1,0:T(8,128)} %eval_jaxpr.5), calls=%async_computation | async-start | bytes 3145728 | tf_op jit(solution)/shard_map/while/body/eval_jaxpr/all_to_all | solution.py:77
  65.9 18.5 %all-to-all-start.1 = ((bf16[128,4,512]{2,1,0:T(4,128)(2,1)}), bf16[128,4,512]{2,1,0:T(4,128)(2,1)S(1)}, u32[]{:S(2)}, u32[]{:S(2)}) async-start(bf16[128,4,512]{2,1,0:T(4,128)(2,1)} %bitcast.99), calls=%async_computation.1 | async-start | bytes 1048576 | tf_op jit(solution)/shard_map/while/body/eval_jaxpr/all_to_all | solution.py:99
  89.5 2.2 %copy-start.7 = (bf16[2,1024,1024]{2,1,0:T(8,128)(2,1)S(1)}, bf16[2,1024,1024]{2,1,0:T(8,128)(2,1)}, u32[]{:S(2)}) copy-start(bf16[2,1024,1024]{2,1,0:T(8,128)(2,1)} %get-tuple-element.317) | copy-start | bytes 12582916 | tf_op jit(solution)/shard_map/while
  95.2 6.0 %copy-start.2 = (bf16[4,256,1024]{2,1,0:T(8,128)(2,1)}, bf16[4,256,1024]{2,1,0:T(8,128)(2,1)S(1)}, u32[]{:S(2)}) copy-start(bf16[4,256,1024]{2,1,0:T(8,128)(2,1)S(1)} %fusion.84) | copy-start | bytes 6291460 | tf_op jit(solution)/shard_map/while
  113.0 29.7 %all-to-all-start = ((f32[128,8,384]{2,1,0:T(8,128)}), f32[128,8,384]{2,1,0:T(8,128)}, u32[]{:S(2)}, u32[]{:S(2)}) async-start(f32[128,8,384]{2,1,0:T(8,128)} %eval_jaxpr.5), calls=%async_computation | async-start | bytes 3145728 | tf_op jit(solution)/shard_map/while/body/eval_jaxpr/all_to_all | solution.py:77
  152.1 18.5 %all-to-all-start.1 = ((bf16[128,4,512]{2,1,0:T(4,128)(2,1)}), bf16[128,4,512]{2,1,0:T(4,128)(2,1)S(1)}, u32[]{:S(2)}, u32[]{:S(2)}) async-start(bf16[128,4,512]{2,1,0:T(4,128)(2,1)} %bitcast.99), calls=%async_computation.1 | async-start | bytes 1048576 | tf_op jit(solution)/shard_map/while/body/eval_jaxpr/all_to_all | solution.py:99
  175.7 2.2 %copy-start.7 = (bf16[2,1024,1024]{2,1,0:T(8,128)(2,1)S(1)}, bf16[2,1024,1024]{2,1,0:T(8,128)(2,1)}, u32[]{:S(2)}) copy-start(bf16[2,1024,1024]{2,1,0:T(8,128)(2,1)} %get-tuple-element.317) | copy-start | bytes 12582916 | tf_op jit(solution)/shard_map/while
  180.4 1.3 copy-start
